TPU v7x, 512 devices: a whole 4x4x16 slice. The times are simulated.
512 devices in a mesh: px: 32 (over y, x, core), py: 16 (over z).
Axes of the slice: x: 4, y: 4, z: 16, core: 2. Of those that a mesh axis runs over, the one named last changes fastest.
Arguments:
- start_vecs: float32 [8192, 64, 128], P(('px', 'py')), may hold values from -6 to 6
- local_tiles: bfloat16 [8192, 4, 128, 128], P(('px', 'py')), may hold values from -0.078125 to 0.078125
- local_cols: int32 [8192, 4], P(('px', 'py')), may hold values from 0 to 15
- halo_tiles: bfloat16 [8192, 128, 128], P(('px', 'py')), may hold values from -0.078125 to 0.078125
- halo_slot: int32 [8192], P(('px', 'py')), may hold values from 0 to 7
- boundary: int32 [2048, 2], P(('px', 'py')), may hold values from 0 to 15
Outputs:
- filtered: float32 [8192, 64, 128], P(('px', 'py'))
- gram_matrix: float32 [64, 64], replicated
Inputs may be any that keep to these rules, and one draw needn't show every extreme that they name: `local_cols`: local block indices within the partition. `boundary`: local block indices within the partition.
All inputs are finite; a program needn't handle non-finite values.
Results may differ from a plain program's by a relative error of at most 0.0055.
Values may be sent and summed in bfloat16 or wider, within the bound.
No kernel may reach another device: no remote copies, remote signals or barrier semaphores. Data moves between devices by JAX's collectives and lax.ppermute only.
A program may use at most 64 MiB of HBM per device.

v0:
```python
import jax
import jax.numpy as jnp
from jax import lax
from jax.sharding import PartitionSpec as P

DEG = 9


def from_behind(value, axis, steps):
    count = lax.axis_size(axis)
    pairs = [(source, (source + steps) % count) for source in range(count)]
    return lax.ppermute(value, axis, pairs)


def operator_apply(current, local_tiles, local_cols, halo_tiles, halo_slot, boundary):
    rounded = current.astype(jnp.bfloat16)
    outgoing = rounded[boundary]
    from_xlow = from_behind(outgoing[0], "px", 1)
    from_xhigh = from_behind(outgoing[1], "px", -1)
    from_ylow = from_behind(outgoing[2], "py", 1)
    from_yhigh = from_behind(outgoing[3], "py", -1)
    received = jnp.concatenate([from_xlow, from_xhigh, from_ylow, from_yhigh], axis=0)
    gathered = rounded[local_cols]
    product = jnp.einsum(
        "rtkj,rtij->rki", gathered, local_tiles, preferred_element_type=jnp.float32
    )
    coupled = jnp.einsum(
        "rkj,rij->rki", received[halo_slot], halo_tiles, preferred_element_type=jnp.float32
    )
    return product + coupled


def shards(start_vecs, local_tiles, local_cols, halo_tiles, halo_slot, boundary):

    def step_apply(current):
        return operator_apply(current, local_tiles, local_cols, halo_tiles, halo_slot, boundary)

    first_vecs = step_apply(start_vecs)

    def advance(step_index, state_pair):
        older_vec, newer_vec = state_pair
        return (newer_vec, 2.0 * step_apply(newer_vec) - older_vec)

    previous, current = lax.fori_loop(0, DEG - 1, advance, (start_vecs, first_vecs))
    total_rows = current.shape[0] * current.shape[2] * lax.axis_size("px") * lax.axis_size("py")
    squares = lax.psum(jnp.sum(current * current, axis=(0, 2)), ("px", "py"))
    scales = lax.rsqrt(squares / total_rows + 1e-06)
    filtered = current * scales[None, :, None]
    partial_gram = jnp.einsum("rkj,rlj->kl", filtered, filtered, precision=lax.Precision.HIGHEST)
    gram_matrix = lax.psum(partial_gram, ("px", "py")) / total_rows
    return (filtered, gram_matrix)


def solution(mesh):
    return jax.shard_map(
        shards,
        mesh=mesh,
        in_specs=(
            P(("px", "py"), None, None),
            P(("px", "py"), None, None, None),
            P(("px", "py"), None),
            P(("px", "py"), None, None),
            P(("px", "py")),
            P(("px", "py"), None),
        ),
        out_specs=(P(("px", "py"), None, None), P()),
        check_vma=False,
    )
```

profile of v0, /device:TPU:1, one launch (start us, length us, event | category | flops | bytes accessed | tf_op | source)
XLA Modules:
  0.0 419.5 jit_solution(5818227597087407548)
XLA Ops:
  3.4 4.5 %collective-permute-start.4 = (bf16[2,64,128]{2,1,0:T(8,128)(2,1)S(1)}, bf16[2,64,128]{2,1,0:T(8,128)(2,1)S(1)}, u32[]{:S(2)}, u32[]{:S(2)}) collective-permute-start(bf16[2,64,128]{2,1,0:T(8,128)(2,1)S(1)} %get-tuple-element.65), channel_id=1, source_target_pairs={{0,16},{16,32},{32,48},{48,64},{64,80},{80,96},{96,112},{112,128},... | collective-permute-start | bytes 98312 | tf_op jit(solution)/shard_map/ppermute | solution.py:12
  7.9 3.5 collective-permute-start.6
  11.4 4.5 %collective-permute-start.5 = (bf16[2,64,128]{2,1,0:T(8,128)(2,1)S(1)}, bf16[2,64,128]{2,1,0:T(8,128)(2,1)S(1)}, u32[]{:S(2)}, u32[]{:S(2)}) collective-permute-start(bf16[2,64,128]{2,1,0:T(8,128)(2,1)S(1)} %get-tuple-element.67), channel_id=1, source_target_pairs={{0,496},{16,0},{32,16},{48,32},{64,48},{80,64},{96,80},{112,96},{1... | collective-permute-start | bytes 98312 | tf_op jit(solution)/shard_map/ppermute | solution.py:12
  16.0 6.9 %collective-permute-start.7 = (bf16[2,64,128]{2,1,0:T(8,128)(2,1)S(1)}, bf16[2,64,128]{2,1,0:T(8,128)(2,1)S(1)}, u32[]{:S(2)}, u32[]{:S(2)}) collective-permute-start(bf16[2,64,128]{2,1,0:T(8,128)(2,1)S(1)} %get-tuple-element.68), channel_id=1, source_target_pairs={{0,15},{1,0},{2,1},{3,2},{4,3},{5,4},{6,5},{7,6},{8,7},{9,8},{10,9... | collective-permute-start | bytes 98312 | tf_op jit(solution)/shard_map/ppermute | solution.py:12
  24.8 2.9 convolution_bitcast_fusion.1
  29.9 184.2 %while.12 = (s32[]{:T(128)}, f32[16,64,128]{2,1,0:T(8,128)}, f32[16,64,128]{2,1,0:T(8,128)S(1)}, s32[16,4]{0,1:T(4,128)S(1)}, bf16[16,4,128,128]{3,2,1,0:T(8,128...) while((s32[]{:T(128)}, f32[16,64,128]{2,1,0:T(8,128)}, ...), condition=%wide.region_1.0_spmd, body=%wide.region_0.0_spmd.sunk | while | flops 168496400 | bytes 23345988 | solution.py:44
  30.8 3.4 collective-permute-start
  34.1 1.9 collective-permute-start.1
  36.1 6.7 %collective-permute-start.2 = (bf16[2,64,128]{2,1,0:T(8,128)(2,1)S(1)}, bf16[2,64,128]{2,1,0:T(8,128)(2,1)S(1)}, u32[]{:S(2)}, u32[]{:S(2)}) collective-permute-start(bf16[2,64,128]{2,1,0:T(8,128)(2,1)S(1)} %get-tuple-element.124), channel_id=1, source_target_pairs={{0,496},{16,0},{32,16},{48,32},{64,48},{80,64},{96,80},{112,96},{1... | collective-permute-start | bytes 98312 | tf_op jit(solution)/shard_map/while/body/eval_jaxpr/ppermute | solution.py:12
  42.8 1.9 collective-permute-start.3
  45.7 2.4 convolution_bitcast_fusion.4
  52.7 4.6 %collective-permute-start = (bf16[2,64,128]{2,1,0:T(8,128)(2,1)S(1)}, bf16[2,64,128]{2,1,0:T(8,128)(2,1)S(1)}, u32[]{:S(2)}, u32[]{:S(2)}) collective-permute-start(bf16[2,64,128]{2,1,0:T(8,128)(2,1)S(1)} %get-tuple-element.122), channel_id=1, source_target_pairs={{0,15},{1,0},{2,1},{3,2},{4,3},{5,4},{6,5},{7,6},{8,7},{9,8},{10,9... | collective-permute-start | bytes 98312 | tf_op jit(solution)/shard_map/while/body/eval_jaxpr/ppermute | solution.py:12
  57.3 1.9 collective-permute-start.1
  59.2 5.4 %collective-permute-start.2 = (bf16[2,64,128]{2,1,0:T(8,128)(2,1)S(1)}, bf16[2,64,128]{2,1,0:T(8,128)(2,1)S(1)}, u32[]{:S(2)}, u32[]{:S(2)}) collective-permute-start(bf16[2,64,128]{2,1,0:T(8,128)(2,1)S(1)} %get-tuple-element.124), channel_id=1, source_target_pairs={{0,496},{16,0},{32,16},{48,32},{64,48},{80,64},{96,80},{112,96},{1... | collective-permute-start | bytes 98312 | tf_op jit(solution)/shard_map/while/body/eval_jaxpr/ppermute | solution.py:12
  64.6 1.9 collective-permute-start.3
  67.5 2.4 convolution_bitcast_fusion.4
  74.5 4.9 %collective-permute-start = (bf16[2,64,128]{2,1,0:T(8,128)(2,1)S(1)}, bf16[2,64,128]{2,1,0:T(8,128)(2,1)S(1)}, u32[]{:S(2)}, u32[]{:S(2)}) collective-permute-start(bf16[2,64,128]{2,1,0:T(8,128)(2,1)S(1)} %get-tuple-element.122), channel_id=1, source_target_pairs={{0,15},{1,0},{2,1},{3,2},{4,3},{5,4},{6,5},{7,6},{8,7},{9,8},{10,9... | collective-permute-start | bytes 98312 | tf_op jit(solution)/shard_map/while/body/eval_jaxpr/ppermute | solution.py:12
  79.4 1.9 collective-permute-start.1
  81.3 6.7 %collective-permute-start.2 = (bf16[2,64,128]{2,1,0:T(8,128)(2,1)S(1)}, bf16[2,64,128]{2,1,0:T(8,128)(2,1)S(1)}, u32[]{:S(2)}, u32[]{:S(2)}) collective-permute-start(bf16[2,64,128]{2,1,0:T(8,128)(2,1)S(1)} %get-tuple-element.124), channel_id=1, source_target_pairs={{0,496},{16,0},{32,16},{48,32},{64,48},{80,64},{96,80},{112,96},{1... | collective-permute-start | bytes 98312 | tf_op jit(solution)/shard_map/while/body/eval_jaxpr/ppermute | solution.py:12
  88.0 1.9 collective-permute-start.3
  90.9 2.4 convolution_bitcast_fusion.4
  97.9 4.8 %collective-permute-start = (bf16[2,64,128]{2,1,0:T(8,128)(2,1)S(1)}, bf16[2,64,128]{2,1,0:T(8,128)(2,1)S(1)}, u32[]{:S(2)}, u32[]{:S(2)}) collective-permute-start(bf16[2,64,128]{2,1,0:T(8,128)(2,1)S(1)} %get-tuple-element.122), channel_id=1, source_target_pairs={{0,15},{1,0},{2,1},{3,2},{4,3},{5,4},{6,5},{7,6},{8,7},{9,8},{10,9... | collective-permute-start | bytes 98312 | tf_op jit(solution)/shard_map/while/body/eval_jaxpr/ppermute | solution.py:12
  102.8 1.9 collective-permute-start.1
  104.7 6.7 %collective-permute-start.2 = (bf16[2,64,128]{2,1,0:T(8,128)(2,1)S(1)}, bf16[2,64,128]{2,1,0:T(8,128)(2,1)S(1)}, u32[]{:S(2)}, u32[]{:S(2)}) collective-permute-start(bf16[2,64,128]{2,1,0:T(8,128)(2,1)S(1)} %get-tuple-element.124), channel_id=1, source_target_pairs={{0,496},{16,0},{32,16},{48,32},{64,48},{80,64},{96,80},{112,96},{1... | collective-permute-start | bytes 98312 | tf_op jit(solution)/shard_map/while/body/eval_jaxpr/ppermute | solution.py:12
  111.4 1.9 collective-permute-start.3
  114.3 2.4 convolution_bitcast_fusion.4
  121.3 4.9 %collective-permute-start = (bf16[2,64,128]{2,1,0:T(8,128)(2,1)S(1)}, bf16[2,64,128]{2,1,0:T(8,128)(2,1)S(1)}, u32[]{:S(2)}, u32[]{:S(2)}) collective-permute-start(bf16[2,64,128]{2,1,0:T(8,128)(2,1)S(1)} %get-tuple-element.122), channel_id=1, source_target_pairs={{0,15},{1,0},{2,1},{3,2},{4,3},{5,4},{6,5},{7,6},{8,7},{9,8},{10,9... | collective-permute-start | bytes 98312 | tf_op jit(solution)/shard_map/while/body/eval_jaxpr/ppermute | solution.py:12
  126.2 1.9 collective-permute-start.1
  128.1 6.7 %collective-permute-start.2 = (bf16[2,64,128]{2,1,0:T(8,128)(2,1)S(1)}, bf16[2,64,128]{2,1,0:T(8,128)(2,1)S(1)}, u32[]{:S(2)}, u32[]{:S(2)}) collective-permute-start(bf16[2,64,128]{2,1,0:T(8,128)(2,1)S(1)} %get-tuple-element.124), channel_id=1, source_target_pairs={{0,496},{16,0},{32,16},{48,32},{64,48},{80,64},{96,80},{112,96},{1... | collective-permute-start | bytes 98312 | tf_op jit(solution)/shard_map/while/body/eval_jaxpr/ppermute | solution.py:12
  134.8 1.9 collective-permute-start.3
  137.7 2.4 convolution_bitcast_fusion.4
  144.7 4.8 %collective-permute-start = (bf16[2,64,128]{2,1,0:T(8,128)(2,1)S(1)}, bf16[2,64,128]{2,1,0:T(8,128)(2,1)S(1)}, u32[]{:S(2)}, u32[]{:S(2)}) collective-permute-start(bf16[2,64,128]{2,1,0:T(8,128)(2,1)S(1)} %get-tuple-element.122), channel_id=1, source_target_pairs={{0,15},{1,0},{2,1},{3,2},{4,3},{5,4},{6,5},{7,6},{8,7},{9,8},{10,9... | collective-permute-start | bytes 98312 | tf_op jit(solution)/shard_map/while/body/eval_jaxpr/ppermute | solution.py:12
  149.6 1.9 collective-permute-start.1
  151.5 6.7 %collective-permute-start.2 = (bf16[2,64,128]{2,1,0:T(8,128)(2,1)S(1)}, bf16[2,64,128]{2,1,0:T(8,128)(2,1)S(1)}, u32[]{:S(2)}, u32[]{:S(2)}) collective-permute-start(bf16[2,64,128]{2,1,0:T(8,128)(2,1)S(1)} %get-tuple-element.124), channel_id=1, source_target_pairs={{0,496},{16,0},{32,16},{48,32},{64,48},{80,64},{96,80},{112,96},{1... | collective-permute-start | bytes 98312 | tf_op jit(solution)/shard_map/while/body/eval_jaxpr/ppermute | solution.py:12
  158.2 1.9 collective-permute-start.3
  161.1 2.4 convolution_bitcast_fusion.4
  168.2 4.9 %collective-permute-start = (bf16[2,64,128]{2,1,0:T(8,128)(2,1)S(1)}, bf16[2,64,128]{2,1,0:T(8,128)(2,1)S(1)}, u32[]{:S(2)}, u32[]{:S(2)}) collective-permute-start(bf16[2,64,128]{2,1,0:T(8,128)(2,1)S(1)} %get-tuple-element.122), channel_id=1, source_target_pairs={{0,15},{1,0},{2,1},{3,2},{4,3},{5,4},{6,5},{7,6},{8,7},{9,8},{10,9... | collective-permute-start | bytes 98312 | tf_op jit(solution)/shard_map/while/body/eval_jaxpr/ppermute | solution.py:12
  173.0 1.9 collective-permute-start.1
  174.9 6.7 %collective-permute-start.2 = (bf16[2,64,128]{2,1,0:T(8,128)(2,1)S(1)}, bf16[2,64,128]{2,1,0:T(8,128)(2,1)S(1)}, u32[]{:S(2)}, u32[]{:S(2)}) collective-permute-start(bf16[2,64,128]{2,1,0:T(8,128)(2,1)S(1)} %get-tuple-element.124), channel_id=1, source_target_pairs={{0,496},{16,0},{32,16},{48,32},{64,48},{80,64},{96,80},{112,96},{1... | collective-permute-start | bytes 98312 | tf_op jit(solution)/shard_map/while/body/eval_jaxpr/ppermute | solution.py:12
  181.6 1.9 collective-permute-start.3
  184.5 2.4 convolution_bitcast_fusion.4
  191.6 4.8 %collective-permute-start = (bf16[2,64,128]{2,1,0:T(8,128)(2,1)S(1)}, bf16[2,64,128]{2,1,0:T(8,128)(2,1)S(1)}, u32[]{:S(2)}, u32[]{:S(2)}) collective-permute-start(bf16[2,64,128]{2,1,0:T(8,128)(2,1)S(1)} %get-tuple-element.122), channel_id=1, source_target_pairs={{0,15},{1,0},{2,1},{3,2},{4,3},{5,4},{6,5},{7,6},{8,7},{9,8},{10,9... | collective-permute-start | bytes 98312 | tf_op jit(solution)/shard_map/while/body/eval_jaxpr/ppermute | solution.py:12
  196.4 1.9 collective-permute-start.1
  198.3 6.7 %collective-permute-start.2 = (bf16[2,64,128]{2,1,0:T(8,128)(2,1)S(1)}, bf16[2,64,128]{2,1,0:T(8,128)(2,1)S(1)}, u32[]{:S(2)}, u32[]{:S(2)}) collective-permute-start(bf16[2,64,128]{2,1,0:T(8,128)(2,1)S(1)} %get-tuple-element.124), channel_id=1, source_target_pairs={{0,496},{16,0},{32,16},{48,32},{64,48},{80,64},{96,80},{112,96},{1... | collective-permute-start | bytes 98312 | tf_op jit(solution)/shard_map/while/body/eval_jaxpr/ppermute | solution.py:12
  205.0 1.9 collective-permute-start.3
  207.9 2.4 convolution_bitcast_fusion.4
  214.3 105.2 %psum.14 = f32[64]{0:T(128)S(1)} all-reduce(f32[64]{0:T(128)S(1)} %multiply_reduce_fusion), channel_id=1, replica_groups=mesh['px'=32,'py'=16] {'px','py'}, use_global_device_ids=true, to_apply=%region_3.0 | all-reduce | flops 64 | bytes 512 | tf_op jit(solution)/shard_map/psum | solution.py:46
  320.2 98.6 %psum.15 = f32[64,64]{1,0:T(8,128)S(1)} all-reduce(f32[64,64]{1,0:T(8,128)S(1)} %convolution_bitcast_fusion.2), channel_id=1, replica_groups=mesh['px'=32,'py'=16] {'px','py'}, use_global_device_ids=true, to_apply=%region_4.0 | all-reduce | flops 4096 | bytes 32768 | tf_op jit(solution)/shard_map/psum | solution.py:50
  (257 shorter events, 51.5 us)
Async XLA Ops:
  0.6 24.1 %copy-start = (bf16[16,4,128,128]{3,2,1,0:T(8,128)(2,1)S(1)}, bf16[16,4,128,128]{3,2,1,0:T(8,128)(2,1)}, u32[]{:S(2)}) copy-start(bf16[16,4,128,128]{3,2,1,0:T(8,128)(2,1)} %param.9) | copy-start | bytes 6291460
  0.6 22.3 %copy-start.6 = (s32[16,4]{0,1:T(4,128)S(1)}, s32[16,4]{0,1:T(4,128)}, u32[]{:S(2)}) copy-start(s32[16,4]{0,1:T(4,128)} %param.10) | copy-start | bytes 772
  0.7 22.2 %copy-start.8 = (s32[16]{0:T(128)S(1)}, s32[16]{0:T(128)}, u32[]{:S(2)}) copy-start(s32[16]{0:T(128)} %param.12) | copy-start | bytes 196
  1.9 25.8 %copy-start.2 = (f32[16,64,128]{2,1,0:T(8,128)}, f32[16,64,128]{2,1,0:T(8,128)S(1)}, u32[]{:S(2)}) copy-start(f32[16,64,128]{2,1,0:T(8,128)S(1)} %copy.33) | copy-start | bytes 1572868
  3.4 24.3 %collective-permute-start.4 = (bf16[2,64,128]{2,1,0:T(8,128)(2,1)S(1)}, bf16[2,64,128]{2,1,0:T(8,128)(2,1)S(1)}, u32[]{:S(2)}, u32[]{:S(2)}) collective-permute-start(bf16[2,64,128]{2,1,0:T(8,128)(2,1)S(1)} %get-tuple-element.65), channel_id=1, source_target_pairs={{0,16},{16,32},{32,48},{48,64},{64,80},{80,96},{96,112},{112,128},... | collective-permute-start | bytes 98312 | tf_op jit(solution)/shard_map/ppermute | solution.py:12
  7.9 19.8 %collective-permute-start.6 = (bf16[2,64,128]{2,1,0:T(8,128)(2,1)S(1)}, bf16[2,64,128]{2,1,0:T(8,128)(2,1)S(1)}, u32[]{:S(2)}, u32[]{:S(2)}) collective-permute-start(bf16[2,64,128]{2,1,0:T(8,128)(2,1)S(1)} %get-tuple-element.66), channel_id=1, source_target_pairs={{0,1},{1,2},{2,3},{3,4},{4,5},{5,6},{6,7},{7,8},{8,9},{9,10},{10,1... | collective-permute-start | bytes 98312 | tf_op jit(solution)/shard_map/ppermute | solution.py:12
  11.4 16.3 %collective-permute-start.5 = (bf16[2,64,128]{2,1,0:T(8,128)(2,1)S(1)}, bf16[2,64,128]{2,1,0:T(8,128)(2,1)S(1)}, u32[]{:S(2)}, u32[]{:S(2)}) collective-permute-start(bf16[2,64,128]{2,1,0:T(8,128)(2,1)S(1)} %get-tuple-element.67), channel_id=1, source_target_pairs={{0,496},{16,0},{32,16},{48,32},{64,48},{80,64},{96,80},{112,96},{1... | collective-permute-start | bytes 98312 | tf_op jit(solution)/shard_map/ppermute | solution.py:12
  16.0 11.7 %collective-permute-start.7 = (bf16[2,64,128]{2,1,0:T(8,128)(2,1)S(1)}, bf16[2,64,128]{2,1,0:T(8,128)(2,1)S(1)}, u32[]{:S(2)}, u32[]{:S(2)}) collective-permute-start(bf16[2,64,128]{2,1,0:T(8,128)(2,1)S(1)} %get-tuple-element.68), channel_id=1, source_target_pairs={{0,15},{1,0},{2,1},{3,2},{4,3},{5,4},{6,5},{7,6},{8,7},{9,8},{10,9... | collective-permute-start | bytes 98312 | tf_op jit(solution)/shard_map/ppermute | solution.py:12
  24.8 3.6 copy-start.3
  30.8 17.3 %collective-permute-start = (bf16[2,64,128]{2,1,0:T(8,128)(2,1)S(1)}, bf16[2,64,128]{2,1,0:T(8,128)(2,1)S(1)}, u32[]{:S(2)}, u32[]{:S(2)}) collective-permute-start(bf16[2,64,128]{2,1,0:T(8,128)(2,1)S(1)} %get-tuple-element.122), channel_id=1, source_target_pairs={{0,15},{1,0},{2,1},{3,2},{4,3},{5,4},{6,5},{7,6},{8,7},{9,8},{10,9... | collective-permute-start | bytes 98312 | tf_op jit(solution)/shard_map/while/body/eval_jaxpr/ppermute | solution.py:12
  34.1 14.0 %collective-permute-start.1 = (bf16[2,64,128]{2,1,0:T(8,128)(2,1)S(1)}, bf16[2,64,128]{2,1,0:T(8,128)(2,1)S(1)}, u32[]{:S(2)}, u32[]{:S(2)}) collective-permute-start(bf16[2,64,128]{2,1,0:T(8,128)(2,1)S(1)} %get-tuple-element.123), channel_id=1, source_target_pairs={{0,1},{1,2},{2,3},{3,4},{4,5},{5,6},{6,7},{7,8},{8,9},{9,10},{10,1... | collective-permute-start | bytes 98312 | tf_op jit(solution)/shard_map/while/body/eval_jaxpr/ppermute | solution.py:12
  36.1 12.1 %collective-permute-start.2 = (bf16[2,64,128]{2,1,0:T(8,128)(2,1)S(1)}, bf16[2,64,128]{2,1,0:T(8,128)(2,1)S(1)}, u32[]{:S(2)}, u32[]{:S(2)}) collective-permute-start(bf16[2,64,128]{2,1,0:T(8,128)(2,1)S(1)} %get-tuple-element.124), channel_id=1, source_target_pairs={{0,496},{16,0},{32,16},{48,32},{64,48},{80,64},{96,80},{112,96},{1... | collective-permute-start | bytes 98312 | tf_op jit(solution)/shard_map/while/body/eval_jaxpr/ppermute | solution.py:12
  42.8 5.4 %collective-permute-start.3 = (bf16[2,64,128]{2,1,0:T(8,128)(2,1)S(1)}, bf16[2,64,128]{2,1,0:T(8,128)(2,1)S(1)}, u32[]{:S(2)}, u32[]{:S(2)}) collective-permute-start(bf16[2,64,128]{2,1,0:T(8,128)(2,1)S(1)} %get-tuple-element.125), channel_id=1, source_target_pairs={{0,16},{16,32},{32,48},{48,64},{64,80},{80,96},{96,112},{112,128},... | collective-permute-start | bytes 98312 | tf_op jit(solution)/shard_map/while/body/eval_jaxpr/ppermute | solution.py:12
  48.8 2.7 copy-start.1
  52.7 17.2 %collective-permute-start = (bf16[2,64,128]{2,1,0:T(8,128)(2,1)S(1)}, bf16[2,64,128]{2,1,0:T(8,128)(2,1)S(1)}, u32[]{:S(2)}, u32[]{:S(2)}) collective-permute-start(bf16[2,64,128]{2,1,0:T(8,128)(2,1)S(1)} %get-tuple-element.122), channel_id=1, source_target_pairs={{0,15},{1,0},{2,1},{3,2},{4,3},{5,4},{6,5},{7,6},{8,7},{9,8},{10,9... | collective-permute-start | bytes 98312 | tf_op jit(solution)/shard_map/while/body/eval_jaxpr/ppermute | solution.py:12
  57.3 12.7 %collective-permute-start.1 = (bf16[2,64,128]{2,1,0:T(8,128)(2,1)S(1)}, bf16[2,64,128]{2,1,0:T(8,128)(2,1)S(1)}, u32[]{:S(2)}, u32[]{:S(2)}) collective-permute-start(bf16[2,64,128]{2,1,0:T(8,128)(2,1)S(1)} %get-tuple-element.123), channel_id=1, source_target_pairs={{0,1},{1,2},{2,3},{3,4},{4,5},{5,6},{6,7},{7,8},{8,9},{9,10},{10,1... | collective-permute-start | bytes 98312 | tf_op jit(solution)/shard_map/while/body/eval_jaxpr/ppermute | solution.py:12
  59.2 10.7 %collective-permute-start.2 = (bf16[2,64,128]{2,1,0:T(8,128)(2,1)S(1)}, bf16[2,64,128]{2,1,0:T(8,128)(2,1)S(1)}, u32[]{:S(2)}, u32[]{:S(2)}) collective-permute-start(bf16[2,64,128]{2,1,0:T(8,128)(2,1)S(1)} %get-tuple-element.124), channel_id=1, source_target_pairs={{0,496},{16,0},{32,16},{48,32},{64,48},{80,64},{96,80},{112,96},{1... | collective-permute-start | bytes 98312 | tf_op jit(solution)/shard_map/while/body/eval_jaxpr/ppermute | solution.py:12
  64.6 5.4 %collective-permute-start.3 = (bf16[2,64,128]{2,1,0:T(8,128)(2,1)S(1)}, bf16[2,64,128]{2,1,0:T(8,128)(2,1)S(1)}, u32[]{:S(2)}, u32[]{:S(2)}) collective-permute-start(bf16[2,64,128]{2,1,0:T(8,128)(2,1)S(1)} %get-tuple-element.125), channel_id=1, source_target_pairs={{0,16},{16,32},{32,48},{48,64},{64,80},{80,96},{96,112},{112,128},... | collective-permute-start | bytes 98312 | tf_op jit(solution)/shard_map/while/body/eval_jaxpr/ppermute | solution.py:12
  70.6 2.7 copy-start.1
  74.5 18.8 %collective-permute-start = (bf16[2,64,128]{2,1,0:T(8,128)(2,1)S(1)}, bf16[2,64,128]{2,1,0:T(8,128)(2,1)S(1)}, u32[]{:S(2)}, u32[]{:S(2)}) collective-permute-start(bf16[2,64,128]{2,1,0:T(8,128)(2,1)S(1)} %get-tuple-element.122), channel_id=1, source_target_pairs={{0,15},{1,0},{2,1},{3,2},{4,3},{5,4},{6,5},{7,6},{8,7},{9,8},{10,9... | collective-permute-start | bytes 98312 | tf_op jit(solution)/shard_map/while/body/eval_jaxpr/ppermute | solution.py:12
  79.4 14.0 %collective-permute-start.1 = (bf16[2,64,128]{2,1,0:T(8,128)(2,1)S(1)}, bf16[2,64,128]{2,1,0:T(8,128)(2,1)S(1)}, u32[]{:S(2)}, u32[]{:S(2)}) collective-permute-start(bf16[2,64,128]{2,1,0:T(8,128)(2,1)S(1)} %get-tuple-element.123), channel_id=1, source_target_pairs={{0,1},{1,2},{2,3},{3,4},{4,5},{5,6},{6,7},{7,8},{8,9},{9,10},{10,1... | collective-permute-start | bytes 98312 | tf_op jit(solution)/shard_map/while/body/eval_jaxpr/ppermute | solution.py:12
  81.3 12.0 %collective-permute-start.2 = (bf16[2,64,128]{2,1,0:T(8,128)(2,1)S(1)}, bf16[2,64,128]{2,1,0:T(8,128)(2,1)S(1)}, u32[]{:S(2)}, u32[]{:S(2)}) collective-permute-start(bf16[2,64,128]{2,1,0:T(8,128)(2,1)S(1)} %get-tuple-element.124), channel_id=1, source_target_pairs={{0,496},{16,0},{32,16},{48,32},{64,48},{80,64},{96,80},{112,96},{1... | collective-permute-start | bytes 98312 | tf_op jit(solution)/shard_map/while/body/eval_jaxpr/ppermute | solution.py:12
  88.0 5.4 %collective-permute-start.3 = (bf16[2,64,128]{2,1,0:T(8,128)(2,1)S(1)}, bf16[2,64,128]{2,1,0:T(8,128)(2,1)S(1)}, u32[]{:S(2)}, u32[]{:S(2)}) collective-permute-start(bf16[2,64,128]{2,1,0:T(8,128)(2,1)S(1)} %get-tuple-element.125), channel_id=1, source_target_pairs={{0,16},{16,32},{32,48},{48,64},{64,80},{80,96},{96,112},{112,128},... | collective-permute-start | bytes 98312 | tf_op jit(solution)/shard_map/while/body/eval_jaxpr/ppermute | solution.py:12
  94.0 2.7 copy-start.1
  97.9 18.8 %collective-permute-start = (bf16[2,64,128]{2,1,0:T(8,128)(2,1)S(1)}, bf16[2,64,128]{2,1,0:T(8,128)(2,1)S(1)}, u32[]{:S(2)}, u32[]{:S(2)}) collective-permute-start(bf16[2,64,128]{2,1,0:T(8,128)(2,1)S(1)} %get-tuple-element.122), channel_id=1, source_target_pairs={{0,15},{1,0},{2,1},{3,2},{4,3},{5,4},{6,5},{7,6},{8,7},{9,8},{10,9... | collective-permute-start | bytes 98312 | tf_op jit(solution)/shard_map/while/body/eval_jaxpr/ppermute | solution.py:12
  102.8 14.0 %collective-permute-start.1 = (bf16[2,64,128]{2,1,0:T(8,128)(2,1)S(1)}, bf16[2,64,128]{2,1,0:T(8,128)(2,1)S(1)}, u32[]{:S(2)}, u32[]{:S(2)}) collective-permute-start(bf16[2,64,128]{2,1,0:T(8,128)(2,1)S(1)} %get-tuple-element.123), channel_id=1, source_target_pairs={{0,1},{1,2},{2,3},{3,4},{4,5},{5,6},{6,7},{7,8},{8,9},{9,10},{10,1... | collective-permute-start | bytes 98312 | tf_op jit(solution)/shard_map/while/body/eval_jaxpr/ppermute | solution.py:12
  104.7 12.0 %collective-permute-start.2 = (bf16[2,64,128]{2,1,0:T(8,128)(2,1)S(1)}, bf16[2,64,128]{2,1,0:T(8,128)(2,1)S(1)}, u32[]{:S(2)}, u32[]{:S(2)}) collective-permute-start(bf16[2,64,128]{2,1,0:T(8,128)(2,1)S(1)} %get-tuple-element.124), channel_id=1, source_target_pairs={{0,496},{16,0},{32,16},{48,32},{64,48},{80,64},{96,80},{112,96},{1... | collective-permute-start | bytes 98312 | tf_op jit(solution)/shard_map/while/body/eval_jaxpr/ppermute | solution.py:12
  111.4 5.4 %collective-permute-start.3 = (bf16[2,64,128]{2,1,0:T(8,128)(2,1)S(1)}, bf16[2,64,128]{2,1,0:T(8,128)(2,1)S(1)}, u32[]{:S(2)}, u32[]{:S(2)}) collective-permute-start(bf16[2,64,128]{2,1,0:T(8,128)(2,1)S(1)} %get-tuple-element.125), channel_id=1, source_target_pairs={{0,16},{16,32},{32,48},{48,64},{64,80},{80,96},{96,112},{112,128},... | collective-permute-start | bytes 98312 | tf_op jit(solution)/shard_map/while/body/eval_jaxpr/ppermute | solution.py:12
  117.4 2.7 copy-start.1
  121.3 18.8 %collective-permute-start = (bf16[2,64,128]{2,1,0:T(8,128)(2,1)S(1)}, bf16[2,64,128]{2,1,0:T(8,128)(2,1)S(1)}, u32[]{:S(2)}, u32[]{:S(2)}) collective-permute-start(bf16[2,64,128]{2,1,0:T(8,128)(2,1)S(1)} %get-tuple-element.122), channel_id=1, source_target_pairs={{0,15},{1,0},{2,1},{3,2},{4,3},{5,4},{6,5},{7,6},{8,7},{9,8},{10,9... | collective-permute-start | bytes 98312 | tf_op jit(solution)/shard_map/while/body/eval_jaxpr/ppermute | solution.py:12
  126.2 14.0 %collective-permute-start.1 = (bf16[2,64,128]{2,1,0:T(8,128)(2,1)S(1)}, bf16[2,64,128]{2,1,0:T(8,128)(2,1)S(1)}, u32[]{:S(2)}, u32[]{:S(2)}) collective-permute-start(bf16[2,64,128]{2,1,0:T(8,128)(2,1)S(1)} %get-tuple-element.123), channel_id=1, source_target_pairs={{0,1},{1,2},{2,3},{3,4},{4,5},{5,6},{6,7},{7,8},{8,9},{9,10},{10,1... | collective-permute-start | bytes 98312 | tf_op jit(solution)/shard_map/while/body/eval_jaxpr/ppermute | solution.py:12
  128.1 12.0 %collective-permute-start.2 = (bf16[2,64,128]{2,1,0:T(8,128)(2,1)S(1)}, bf16[2,64,128]{2,1,0:T(8,128)(2,1)S(1)}, u32[]{:S(2)}, u32[]{:S(2)}) collective-permute-start(bf16[2,64,128]{2,1,0:T(8,128)(2,1)S(1)} %get-tuple-element.124), channel_id=1, source_target_pairs={{0,496},{16,0},{32,16},{48,32},{64,48},{80,64},{96,80},{112,96},{1... | collective-permute-start | bytes 98312 | tf_op jit(solution)/shard_map/while/body/eval_jaxpr/ppermute | solution.py:12
  134.8 5.4 %collective-permute-start.3 = (bf16[2,64,128]{2,1,0:T(8,128)(2,1)S(1)}, bf16[2,64,128]{2,1,0:T(8,128)(2,1)S(1)}, u32[]{:S(2)}, u32[]{:S(2)}) collective-permute-start(bf16[2,64,128]{2,1,0:T(8,128)(2,1)S(1)} %get-tuple-element.125), channel_id=1, source_target_pairs={{0,16},{16,32},{32,48},{48,64},{64,80},{80,96},{96,112},{112,128},... | collective-permute-start | bytes 98312 | tf_op jit(solution)/shard_map/while/body/eval_jaxpr/ppermute | solution.py:12
  140.8 2.7 copy-start.1
  144.7 18.8 %collective-permute-start = (bf16[2,64,128]{2,1,0:T(8,128)(2,1)S(1)}, bf16[2,64,128]{2,1,0:T(8,128)(2,1)S(1)}, u32[]{:S(2)}, u32[]{:S(2)}) collective-permute-start(bf16[2,64,128]{2,1,0:T(8,128)(2,1)S(1)} %get-tuple-element.122), channel_id=1, source_target_pairs={{0,15},{1,0},{2,1},{3,2},{4,3},{5,4},{6,5},{7,6},{8,7},{9,8},{10,9... | collective-permute-start | bytes 98312 | tf_op jit(solution)/shard_map/while/body/eval_jaxpr/ppermute | solution.py:12
  149.6 14.0 %collective-permute-start.1 = (bf16[2,64,128]{2,1,0:T(8,128)(2,1)S(1)}, bf16[2,64,128]{2,1,0:T(8,128)(2,1)S(1)}, u32[]{:S(2)}, u32[]{:S(2)}) collective-permute-start(bf16[2,64,128]{2,1,0:T(8,128)(2,1)S(1)} %get-tuple-element.123), channel_id=1, source_target_pairs={{0,1},{1,2},{2,3},{3,4},{4,5},{5,6},{6,7},{7,8},{8,9},{9,10},{10,1... | collective-permute-start | bytes 98312 | tf_op jit(solution)/shard_map/while/body/eval_jaxpr/ppermute | solution.py:12
  151.5 12.0 %collective-permute-start.2 = (bf16[2,64,128]{2,1,0:T(8,128)(2,1)S(1)}, bf16[2,64,128]{2,1,0:T(8,128)(2,1)S(1)}, u32[]{:S(2)}, u32[]{:S(2)}) collective-permute-start(bf16[2,64,128]{2,1,0:T(8,128)(2,1)S(1)} %get-tuple-element.124), channel_id=1, source_target_pairs={{0,496},{16,0},{32,16},{48,32},{64,48},{80,64},{96,80},{112,96},{1... | collective-permute-start | bytes 98312 | tf_op jit(solution)/shard_map/while/body/eval_jaxpr/ppermute | solution.py:12
  158.2 5.4 %collective-permute-start.3 = (bf16[2,64,128]{2,1,0:T(8,128)(2,1)S(1)}, bf16[2,64,128]{2,1,0:T(8,128)(2,1)S(1)}, u32[]{:S(2)}, u32[]{:S(2)}) collective-permute-start(bf16[2,64,128]{2,1,0:T(8,128)(2,1)S(1)} %get-tuple-element.125), channel_id=1, source_target_pairs={{0,16},{16,32},{32,48},{48,64},{64,80},{80,96},{96,112},{112,128},... | collective-permute-start | bytes 98312 | tf_op jit(solution)/shard_map/while/body/eval_jaxpr/ppermute | solution.py:12
  168.2 18.8 %collective-permute-start = (bf16[2,64,128]{2,1,0:T(8,128)(2,1)S(1)}, bf16[2,64,128]{2,1,0:T(8,128)(2,1)S(1)}, u32[]{:S(2)}, u32[]{:S(2)}) collective-permute-start(bf16[2,64,128]{2,1,0:T(8,128)(2,1)S(1)} %get-tuple-element.122), channel_id=1, source_target_pairs={{0,15},{1,0},{2,1},{3,2},{4,3},{5,4},{6,5},{7,6},{8,7},{9,8},{10,9... | collective-permute-start | bytes 98312 | tf_op jit(solution)/shard_map/while/body/eval_jaxpr/ppermute | solution.py:12
  173.0 14.0 %collective-permute-start.1 = (bf16[2,64,128]{2,1,0:T(8,128)(2,1)S(1)}, bf16[2,64,128]{2,1,0:T(8,128)(2,1)S(1)}, u32[]{:S(2)}, u32[]{:S(2)}) collective-permute-start(bf16[2,64,128]{2,1,0:T(8,128)(2,1)S(1)} %get-tuple-element.123), channel_id=1, source_target_pairs={{0,1},{1,2},{2,3},{3,4},{4,5},{5,6},{6,7},{7,8},{8,9},{9,10},{10,1... | collective-permute-start | bytes 98312 | tf_op jit(solution)/shard_map/while/body/eval_jaxpr/ppermute | solution.py:12
  174.9 12.0 %collective-permute-start.2 = (bf16[2,64,128]{2,1,0:T(8,128)(2,1)S(1)}, bf16[2,64,128]{2,1,0:T(8,128)(2,1)S(1)}, u32[]{:S(2)}, u32[]{:S(2)}) collective-permute-start(bf16[2,64,128]{2,1,0:T(8,128)(2,1)S(1)} %get-tuple-element.124), channel_id=1, source_target_pairs={{0,496},{16,0},{32,16},{48,32},{64,48},{80,64},{96,80},{112,96},{1... | collective-permute-start | bytes 98312 | tf_op jit(solution)/shard_map/while/body/eval_jaxpr/ppermute | solution.py:12
  181.6 5.4 %collective-permute-start.3 = (bf16[2,64,128]{2,1,0:T(8,128)(2,1)S(1)}, bf16[2,64,128]{2,1,0:T(8,128)(2,1)S(1)}, u32[]{:S(2)}, u32[]{:S(2)}) collective-permute-start(bf16[2,64,128]{2,1,0:T(8,128)(2,1)S(1)} %get-tuple-element.125), channel_id=1, source_target_pairs={{0,16},{16,32},{32,48},{48,64},{64,80},{80,96},{96,112},{112,128},... | collective-permute-start | bytes 98312 | tf_op jit(solution)/shard_map/while/body/eval_jaxpr/ppermute | solution.py:12
  187.6 2.7 copy-start.1
  191.6 18.8 %collective-permute-start = (bf16[2,64,128]{2,1,0:T(8,128)(2,1)S(1)}, bf16[2,64,128]{2,1,0:T(8,128)(2,1)S(1)}, u32[]{:S(2)}, u32[]{:S(2)}) collective-permute-start(bf16[2,64,128]{2,1,0:T(8,128)(2,1)S(1)} %get-tuple-element.122), channel_id=1, source_target_pairs={{0,15},{1,0},{2,1},{3,2},{4,3},{5,4},{6,5},{7,6},{8,7},{9,8},{10,9... | collective-permute-start | bytes 98312 | tf_op jit(solution)/shard_map/while/body/eval_jaxpr/ppermute | solution.py:12
  196.4 14.0 %collective-permute-start.1 = (bf16[2,64,128]{2,1,0:T(8,128)(2,1)S(1)}, bf16[2,64,128]{2,1,0:T(8,128)(2,1)S(1)}, u32[]{:S(2)}, u32[]{:S(2)}) collective-permute-start(bf16[2,64,128]{2,1,0:T(8,128)(2,1)S(1)} %get-tuple-element.123), channel_id=1, source_target_pairs={{0,1},{1,2},{2,3},{3,4},{4,5},{5,6},{6,7},{7,8},{8,9},{9,10},{10,1... | collective-permute-start | bytes 98312 | tf_op jit(solution)/shard_map/while/body/eval_jaxpr/ppermute | solution.py:12
  198.3 12.0 %collective-permute-start.2 = (bf16[2,64,128]{2,1,0:T(8,128)(2,1)S(1)}, bf16[2,64,128]{2,1,0:T(8,128)(2,1)S(1)}, u32[]{:S(2)}, u32[]{:S(2)}) collective-permute-start(bf16[2,64,128]{2,1,0:T(8,128)(2,1)S(1)} %get-tuple-element.124), channel_id=1, source_target_pairs={{0,496},{16,0},{32,16},{48,32},{64,48},{80,64},{96,80},{112,96},{1... | collective-permute-start | bytes 98312 | tf_op jit(solution)/shard_map/while/body/eval_jaxpr/ppermute | solution.py:12
  205.0 5.4 %collective-permute-start.3 = (bf16[2,64,128]{2,1,0:T(8,128)(2,1)S(1)}, bf16[2,64,128]{2,1,0:T(8,128)(2,1)S(1)}, u32[]{:S(2)}, u32[]{:S(2)}) collective-permute-start(bf16[2,64,128]{2,1,0:T(8,128)(2,1)S(1)} %get-tuple-element.125), channel_id=1, source_target_pairs={{0,16},{16,32},{32,48},{48,64},{64,80},{80,96},{96,112},{112,128},... | collective-permute-start | bytes 98312 | tf_op jit(solution)/shard_map/while/body/eval_jaxpr/ppermute | solution.py:12
  319.6 99.8 %copy-start.5 = (f32[16,64,128]{2,1,0:T(8,128)}, f32[16,64,128]{2,1,0:T(8,128)S(1)}, u32[]{:S(2)}) copy-start(f32[16,64,128]{2,1,0:T(8,128)S(1)} %broadcast_multiply_fusion) | copy-start | bytes 1572868
  (11 other events, 17.6 us)
where the time goes:
time: 421 us; the launch traced here: 419 us
  blocking collectives  204 us (48%)
  starting transfers between devices  139 us (33%)
  matrix products  38.8 us (9%)
  local copies, waits for them, and re-layouts  32.5 us (8%)
    ppermute x36, starting transfers between devices, from_behind(): return lax.ppermute(value, axis, pairs)  139 us
    psum x1, blocking collectives, shards(): squares = lax.psum(jnp.sum(current * current, axis=(0, 2)), ('px', 'py'))  105 us
    psum x1, blocking collectives, shards(): gram_matrix = lax.psum(partial_gram, ('px', 'py')) / total_rows  98.6 us
    dot_general x9, matrix products, operator_apply(): jnp.einsum('rtkj,rtij->rki', gathered, local_tiles, preferred_element_typ...  22.3 us
    dot_general x9, matrix products, operator_apply(): jnp.einsum('rkj,rij->rki', received[halo_slot], halo_tiles, preferred_ele...  16 us
    while x48, local copies, waits for them, and re-layouts  9.86 us
  transfers between devices with their start and end apart: 36, of which 0 were waited for; matrix products, arithmetic and copies ran while one was open for 8% of the time, Pallas kernels for 0%

commit v1 on v0

--- a/solution.py
+++ b/solution.py
@@ -2,8 +2,13 @@
 import jax.numpy as jnp
 from jax import lax
 from jax.sharding import PartitionSpec as P
+from jax.lax import all_gather
 
 DEG = 9
+
+
+def pair_pieces_all(inputs, chip_axis):
+    return all_gather(inputs, chip_axis).sum(axis=0)
 
 
 def from_behind(value, axis, steps):
@@ -43,7 +48,7 @@
 
     previous, current = lax.fori_loop(0, DEG - 1, advance, (start_vecs, first_vecs))
     total_rows = current.shape[0] * current.shape[2] * lax.axis_size("px") * lax.axis_size("py")
-    squares = lax.psum(jnp.sum(current * current, axis=(0, 2)), ("px", "py"))
+    squares = pair_pieces_all(jnp.sum(current * current, axis=(0, 2)), ("px", "py"))
     scales = lax.rsqrt(squares / total_rows + 1e-06)
     filtered = current * scales[None, :, None]
     partial_gram = jnp.einsum("rkj,rlj->kl", filtered, filtered, precision=lax.Precision.HIGHEST)

time: 421 us -> 787 us (1.87)
  waiting for transfers between devices: 0.09 us -> 454 us
  blocking collectives: 204 us -> 99.8 us
  between operations: 0.85 us -> 14.3 us
    unnamed x0 -> x2, waiting for transfers between devices: none -> 454 us
    psum x1 -> x0, blocking collectives: 105 us -> none  [shards(): squares = lax.psum(jnp.sum(current * current, axis=(0, 2)), ('px', 'py'))]
  transfers between devices with their start and end apart: 36 -> 37, of which waited for: 0 -> 1; matrix products, arithmetic and copies ran while one was open for 8% -> 4% of each run, Pallas kernels for 0% -> 0%
where the time goes in v1:
time: 787 us; the launch traced here: 785 us
  waiting for transfers between devices  454 us (58%)
  starting transfers between devices  140 us (18%)
  blocking collectives  99.8 us (13%)
  matrix products  38.8 us (5%)
  local copies, waits for them, and re-layouts  34.4 us (4%)
  between operations  14.3 us (2%)
    unnamed x2, waiting for transfers between devices  454 us
    ppermute x36, starting transfers between devices, from_behind(): return lax.ppermute(value, axis, pairs)  140 us
    psum x1, blocking collectives, shards(): gram_matrix = lax.psum(partial_gram, ('px', 'py')) / total_rows  99.8 us
    dot_general x9, matrix products, operator_apply(): jnp.einsum('rtkj,rtij->rki', gathered, local_tiles, preferred_element_typ...  22.2 us
    dot_general x9, matrix products, operator_apply(): jnp.einsum('rkj,rij->rki', received[halo_slot], halo_tiles, preferred_ele...  16 us
  transfers between devices with their start and end apart: 37, of which 1 were waited for; matrix products, arithmetic and copies ran while one was open for 4% of the time, Pallas kernels for 0%

profile of v1, /device:TPU:1, one launch (start us, length us, event | category | flops | bytes accessed | tf_op | source)
XLA Modules:
  0.0 785.4 jit_solution(10212264804263700301)
XLA Ops:
  10.0 4.5 collective-permute-start.4
  14.5 6.2 collective-permute-start.5
  20.7 1.9 collective-permute-start.6
  22.6 6.9 collective-permute-start.7
  31.4 2.9 convolution_bitcast_fusion.1
  36.5 184.5 %while.12 = (s32[]{:T(128)}, f32[16,64,128]{2,1,0:T(8,128)}, f32[16,64,128]{2,1,0:T(8,128)S(1)}, s32[16,4]{0,1:T(4,128)S(1)}, bf16[16,4,128,128]{3,2,1,0:T(8,128...) while((s32[]{:T(128)}, f32[16,64,128]{2,1,0:T(8,128)}, ...), condition=%wide.region_1.0_spmd, body=%wide.region_0.0_spmd.sunk | while | flops 168496400 | bytes 23345988 | solution.py:49
  37.4 3.4 collective-permute-start
  40.7 1.9 collective-permute-start.1
  42.7 6.7 collective-permute-start.2
  49.4 1.9 collective-permute-start.3
  52.3 2.4 convolution_bitcast_fusion.4
  59.3 4.9 collective-permute-start
  64.2 1.9 collective-permute-start.1
  66.1 5.4 collective-permute-start.2
  71.5 1.9 collective-permute-start.3
  74.4 2.4 convolution_bitcast_fusion.4
  81.4 4.9 collective-permute-start
  86.3 1.9 collective-permute-start.1
  88.2 6.7 collective-permute-start.2
  94.9 1.9 collective-permute-start.3
  97.8 2.4 convolution_bitcast_fusion.4
  104.8 4.9 collective-permute-start
  109.7 1.9 collective-permute-start.1
  111.6 6.7 collective-permute-start.2
  118.3 1.9 collective-permute-start.3
  121.2 2.4 convolution_bitcast_fusion.4
  128.2 4.9 collective-permute-start
  133.1 1.9 collective-permute-start.1
  135.0 6.7 collective-permute-start.2
  141.7 1.9 collective-permute-start.3
  144.6 2.4 convolution_bitcast_fusion.4
  151.6 4.9 collective-permute-start
  156.5 1.9 collective-permute-start.1
  158.4 6.7 collective-permute-start.2
  165.1 1.9 collective-permute-start.3
  168.0 2.4 convolution_bitcast_fusion.4
  175.1 4.9 collective-permute-start
  179.9 1.9 collective-permute-start.1
  181.8 6.7 collective-permute-start.2
  188.5 1.9 collective-permute-start.3
  191.4 2.4 convolution_bitcast_fusion.4
  198.5 4.9 collective-permute-start
  203.3 1.9 collective-permute-start.1
  205.3 6.7 collective-permute-start.2
  211.9 1.9 collective-permute-start.3
  214.8 2.4 convolution_bitcast_fusion.4
  222.1 454.2 %all-reduce.3.cloned.1.call-done = f32[32768]{0:T(1024)} async-done(((f32[32768]{0:T(1024)}), f32[32768]{0:T(1024)}) %all-reduce.3.cloned.1.call-update) | async-done | bytes 131088
  678.2 99.8 %psum.7 = f32[64,64]{1,0:T(8,128)S(1)} all-reduce(f32[64,64]{1,0:T(8,128)S(1)} %convolution_bitcast_fusion.2), channel_id=1, replica_groups=mesh['px'=32,'py'=16] {'px','py'}, use_global_device_ids=true, to_apply=%region_4.0 | all-reduce | flops 4096 | bytes 32768 | tf_op jit(solution)/shard_map/psum | solution.py:55
  (265 shorter events, 53.6 us)
Async XLA Ops:
  7.2 24.2 %copy-start = (bf16[16,4,128,128]{3,2,1,0:T(8,128)(2,1)S(1)}, bf16[16,4,128,128]{3,2,1,0:T(8,128)(2,1)}, u32[]{:S(2)}) copy-start(bf16[16,4,128,128]{3,2,1,0:T(8,128)(2,1)} %param.9) | copy-start | bytes 6291460
  7.2 22.3 %copy-start.7 = (s32[16,4]{0,1:T(4,128)S(1)}, s32[16,4]{0,1:T(4,128)}, u32[]{:S(2)}) copy-start(s32[16,4]{0,1:T(4,128)} %param.10) | copy-start | bytes 772
  7.2 22.3 %copy-start.9 = (s32[16]{0:T(128)S(1)}, s32[16]{0:T(128)}, u32[]{:S(2)}) copy-start(s32[16]{0:T(128)} %param.12) | copy-start | bytes 196
  7.2 669.2 %all-reduce.3.cloned.1.call-start = ((), (), s32[]{:S(2)}) async-start(), calls=%async_computation | async-start | bytes 262144
  8.4 25.9 %copy-start.2 = (f32[16,64,128]{2,1,0:T(8,128)}, f32[16,64,128]{2,1,0:T(8,128)S(1)}, u32[]{:S(2)}) copy-start(f32[16,64,128]{2,1,0:T(8,128)S(1)} %copy.35) | copy-start | bytes 1572868
  10.0 24.3 %collective-permute-start.4 = (bf16[2,64,128]{2,1,0:T(8,128)(2,1)S(1)}, bf16[2,64,128]{2,1,0:T(8,128)(2,1)S(1)}, u32[]{:S(2)}, u32[]{:S(2)}) collective-permute-start(bf16[2,64,128]{2,1,0:T(8,128)(2,1)S(1)} %get-tuple-element.65), channel_id=1, source_target_pairs={{0,16},{16,32},{32,48},{48,64},{64,80},{80,96},{96,112},{112,128},... | collective-permute-start | bytes 98312 | tf_op jit(solution)/shard_map/ppermute | solution.py:17
  14.5 19.8 %collective-permute-start.5 = (bf16[2,64,128]{2,1,0:T(8,128)(2,1)S(1)}, bf16[2,64,128]{2,1,0:T(8,128)(2,1)S(1)}, u32[]{:S(2)}, u32[]{:S(2)}) collective-permute-start(bf16[2,64,128]{2,1,0:T(8,128)(2,1)S(1)} %get-tuple-element.67), channel_id=1, source_target_pairs={{0,496},{16,0},{32,16},{48,32},{64,48},{80,64},{96,80},{112,96},{1... | collective-permute-start | bytes 98312 | tf_op jit(solution)/shard_map/ppermute | solution.py:17
  20.7 13.7 %collective-permute-start.6 = (bf16[2,64,128]{2,1,0:T(8,128)(2,1)S(1)}, bf16[2,64,128]{2,1,0:T(8,128)(2,1)S(1)}, u32[]{:S(2)}, u32[]{:S(2)}) collective-permute-start(bf16[2,64,128]{2,1,0:T(8,128)(2,1)S(1)} %get-tuple-element.66), channel_id=1, source_target_pairs={{0,1},{1,2},{2,3},{3,4},{4,5},{5,6},{6,7},{7,8},{8,9},{9,10},{10,1... | collective-permute-start | bytes 98312 | tf_op jit(solution)/shard_map/ppermute | solution.py:17
  22.6 11.8 %collective-permute-start.7 = (bf16[2,64,128]{2,1,0:T(8,128)(2,1)S(1)}, bf16[2,64,128]{2,1,0:T(8,128)(2,1)S(1)}, u32[]{:S(2)}, u32[]{:S(2)}) collective-permute-start(bf16[2,64,128]{2,1,0:T(8,128)(2,1)S(1)} %get-tuple-element.68), channel_id=1, source_target_pairs={{0,15},{1,0},{2,1},{3,2},{4,3},{5,4},{6,5},{7,6},{8,7},{9,8},{10,9... | collective-permute-start | bytes 98312 | tf_op jit(solution)/shard_map/ppermute | solution.py:17
  31.4 3.6 copy-start.3
  37.4 17.3 %collective-permute-start = (bf16[2,64,128]{2,1,0:T(8,128)(2,1)S(1)}, bf16[2,64,128]{2,1,0:T(8,128)(2,1)S(1)}, u32[]{:S(2)}, u32[]{:S(2)}) collective-permute-start(bf16[2,64,128]{2,1,0:T(8,128)(2,1)S(1)} %get-tuple-element.122), channel_id=1, source_target_pairs={{0,15},{1,0},{2,1},{3,2},{4,3},{5,4},{6,5},{7,6},{8,7},{9,8},{10,9... | collective-permute-start | bytes 98312 | tf_op jit(solution)/shard_map/while/body/eval_jaxpr/ppermute | solution.py:17
  40.7 14.0 %collective-permute-start.1 = (bf16[2,64,128]{2,1,0:T(8,128)(2,1)S(1)}, bf16[2,64,128]{2,1,0:T(8,128)(2,1)S(1)}, u32[]{:S(2)}, u32[]{:S(2)}) collective-permute-start(bf16[2,64,128]{2,1,0:T(8,128)(2,1)S(1)} %get-tuple-element.123), channel_id=1, source_target_pairs={{0,1},{1,2},{2,3},{3,4},{4,5},{5,6},{6,7},{7,8},{8,9},{9,10},{10,1... | collective-permute-start | bytes 98312 | tf_op jit(solution)/shard_map/while/body/eval_jaxpr/ppermute | solution.py:17
  42.7 12.1 %collective-permute-start.2 = (bf16[2,64,128]{2,1,0:T(8,128)(2,1)S(1)}, bf16[2,64,128]{2,1,0:T(8,128)(2,1)S(1)}, u32[]{:S(2)}, u32[]{:S(2)}) collective-permute-start(bf16[2,64,128]{2,1,0:T(8,128)(2,1)S(1)} %get-tuple-element.124), channel_id=1, source_target_pairs={{0,496},{16,0},{32,16},{48,32},{64,48},{80,64},{96,80},{112,96},{1... | collective-permute-start | bytes 98312 | tf_op jit(solution)/shard_map/while/body/eval_jaxpr/ppermute | solution.py:17
  49.4 5.4 collective-permute-start.3
  55.4 2.7 copy-start.1
  59.3 17.5 %collective-permute-start = (bf16[2,64,128]{2,1,0:T(8,128)(2,1)S(1)}, bf16[2,64,128]{2,1,0:T(8,128)(2,1)S(1)}, u32[]{:S(2)}, u32[]{:S(2)}) collective-permute-start(bf16[2,64,128]{2,1,0:T(8,128)(2,1)S(1)} %get-tuple-element.122), channel_id=1, source_target_pairs={{0,15},{1,0},{2,1},{3,2},{4,3},{5,4},{6,5},{7,6},{8,7},{9,8},{10,9... | collective-permute-start | bytes 98312 | tf_op jit(solution)/shard_map/while/body/eval_jaxpr/ppermute | solution.py:17
  64.2 12.7 %collective-permute-start.1 = (bf16[2,64,128]{2,1,0:T(8,128)(2,1)S(1)}, bf16[2,64,128]{2,1,0:T(8,128)(2,1)S(1)}, u32[]{:S(2)}, u32[]{:S(2)}) collective-permute-start(bf16[2,64,128]{2,1,0:T(8,128)(2,1)S(1)} %get-tuple-element.123), channel_id=1, source_target_pairs={{0,1},{1,2},{2,3},{3,4},{4,5},{5,6},{6,7},{7,8},{8,9},{9,10},{10,1... | collective-permute-start | bytes 98312 | tf_op jit(solution)/shard_map/while/body/eval_jaxpr/ppermute | solution.py:17
  66.1 10.7 %collective-permute-start.2 = (bf16[2,64,128]{2,1,0:T(8,128)(2,1)S(1)}, bf16[2,64,128]{2,1,0:T(8,128)(2,1)S(1)}, u32[]{:S(2)}, u32[]{:S(2)}) collective-permute-start(bf16[2,64,128]{2,1,0:T(8,128)(2,1)S(1)} %get-tuple-element.124), channel_id=1, source_target_pairs={{0,496},{16,0},{32,16},{48,32},{64,48},{80,64},{96,80},{112,96},{1... | collective-permute-start | bytes 98312 | tf_op jit(solution)/shard_map/while/body/eval_jaxpr/ppermute | solution.py:17
  71.5 5.4 collective-permute-start.3
  77.5 2.7 copy-start.1
  81.4 18.8 %collective-permute-start = (bf16[2,64,128]{2,1,0:T(8,128)(2,1)S(1)}, bf16[2,64,128]{2,1,0:T(8,128)(2,1)S(1)}, u32[]{:S(2)}, u32[]{:S(2)}) collective-permute-start(bf16[2,64,128]{2,1,0:T(8,128)(2,1)S(1)} %get-tuple-element.122), channel_id=1, source_target_pairs={{0,15},{1,0},{2,1},{3,2},{4,3},{5,4},{6,5},{7,6},{8,7},{9,8},{10,9... | collective-permute-start | bytes 98312 | tf_op jit(solution)/shard_map/while/body/eval_jaxpr/ppermute | solution.py:17
  86.3 14.0 %collective-permute-start.1 = (bf16[2,64,128]{2,1,0:T(8,128)(2,1)S(1)}, bf16[2,64,128]{2,1,0:T(8,128)(2,1)S(1)}, u32[]{:S(2)}, u32[]{:S(2)}) collective-permute-start(bf16[2,64,128]{2,1,0:T(8,128)(2,1)S(1)} %get-tuple-element.123), channel_id=1, source_target_pairs={{0,1},{1,2},{2,3},{3,4},{4,5},{5,6},{6,7},{7,8},{8,9},{9,10},{10,1... | collective-permute-start | bytes 98312 | tf_op jit(solution)/shard_map/while/body/eval_jaxpr/ppermute | solution.py:17
  88.2 12.0 %collective-permute-start.2 = (bf16[2,64,128]{2,1,0:T(8,128)(2,1)S(1)}, bf16[2,64,128]{2,1,0:T(8,128)(2,1)S(1)}, u32[]{:S(2)}, u32[]{:S(2)}) collective-permute-start(bf16[2,64,128]{2,1,0:T(8,128)(2,1)S(1)} %get-tuple-element.124), channel_id=1, source_target_pairs={{0,496},{16,0},{32,16},{48,32},{64,48},{80,64},{96,80},{112,96},{1... | collective-permute-start | bytes 98312 | tf_op jit(solution)/shard_map/while/body/eval_jaxpr/ppermute | solution.py:17
  94.9 5.4 collective-permute-start.3
  104.8 18.8 %collective-permute-start = (bf16[2,64,128]{2,1,0:T(8,128)(2,1)S(1)}, bf16[2,64,128]{2,1,0:T(8,128)(2,1)S(1)}, u32[]{:S(2)}, u32[]{:S(2)}) collective-permute-start(bf16[2,64,128]{2,1,0:T(8,128)(2,1)S(1)} %get-tuple-element.122), channel_id=1, source_target_pairs={{0,15},{1,0},{2,1},{3,2},{4,3},{5,4},{6,5},{7,6},{8,7},{9,8},{10,9... | collective-permute-start | bytes 98312 | tf_op jit(solution)/shard_map/while/body/eval_jaxpr/ppermute | solution.py:17
  109.7 14.0 %collective-permute-start.1 = (bf16[2,64,128]{2,1,0:T(8,128)(2,1)S(1)}, bf16[2,64,128]{2,1,0:T(8,128)(2,1)S(1)}, u32[]{:S(2)}, u32[]{:S(2)}) collective-permute-start(bf16[2,64,128]{2,1,0:T(8,128)(2,1)S(1)} %get-tuple-element.123), channel_id=1, source_target_pairs={{0,1},{1,2},{2,3},{3,4},{4,5},{5,6},{6,7},{7,8},{8,9},{9,10},{10,1... | collective-permute-start | bytes 98312 | tf_op jit(solution)/shard_map/while/body/eval_jaxpr/ppermute | solution.py:17
  111.6 12.0 %collective-permute-start.2 = (bf16[2,64,128]{2,1,0:T(8,128)(2,1)S(1)}, bf16[2,64,128]{2,1,0:T(8,128)(2,1)S(1)}, u32[]{:S(2)}, u32[]{:S(2)}) collective-permute-start(bf16[2,64,128]{2,1,0:T(8,128)(2,1)S(1)} %get-tuple-element.124), channel_id=1, source_target_pairs={{0,496},{16,0},{32,16},{48,32},{64,48},{80,64},{96,80},{112,96},{1... | collective-permute-start | bytes 98312 | tf_op jit(solution)/shard_map/while/body/eval_jaxpr/ppermute | solution.py:17
  118.3 5.4 collective-permute-start.3
  124.3 2.7 copy-start.1
  128.2 18.8 %collective-permute-start = (bf16[2,64,128]{2,1,0:T(8,128)(2,1)S(1)}, bf16[2,64,128]{2,1,0:T(8,128)(2,1)S(1)}, u32[]{:S(2)}, u32[]{:S(2)}) collective-permute-start(bf16[2,64,128]{2,1,0:T(8,128)(2,1)S(1)} %get-tuple-element.122), channel_id=1, source_target_pairs={{0,15},{1,0},{2,1},{3,2},{4,3},{5,4},{6,5},{7,6},{8,7},{9,8},{10,9... | collective-permute-start | bytes 98312 | tf_op jit(solution)/shard_map/while/body/eval_jaxpr/ppermute | solution.py:17
  133.1 14.0 %collective-permute-start.1 = (bf16[2,64,128]{2,1,0:T(8,128)(2,1)S(1)}, bf16[2,64,128]{2,1,0:T(8,128)(2,1)S(1)}, u32[]{:S(2)}, u32[]{:S(2)}) collective-permute-start(bf16[2,64,128]{2,1,0:T(8,128)(2,1)S(1)} %get-tuple-element.123), channel_id=1, source_target_pairs={{0,1},{1,2},{2,3},{3,4},{4,5},{5,6},{6,7},{7,8},{8,9},{9,10},{10,1... | collective-permute-start | bytes 98312 | tf_op jit(solution)/shard_map/while/body/eval_jaxpr/ppermute | solution.py:17
  135.0 12.0 %collective-permute-start.2 = (bf16[2,64,128]{2,1,0:T(8,128)(2,1)S(1)}, bf16[2,64,128]{2,1,0:T(8,128)(2,1)S(1)}, u32[]{:S(2)}, u32[]{:S(2)}) collective-permute-start(bf16[2,64,128]{2,1,0:T(8,128)(2,1)S(1)} %get-tuple-element.124), channel_id=1, source_target_pairs={{0,496},{16,0},{32,16},{48,32},{64,48},{80,64},{96,80},{112,96},{1... | collective-permute-start | bytes 98312 | tf_op jit(solution)/shard_map/while/body/eval_jaxpr/ppermute | solution.py:17
  141.7 5.4 collective-permute-start.3
  147.7 2.7 copy-start.1
  151.6 18.8 %collective-permute-start = (bf16[2,64,128]{2,1,0:T(8,128)(2,1)S(1)}, bf16[2,64,128]{2,1,0:T(8,128)(2,1)S(1)}, u32[]{:S(2)}, u32[]{:S(2)}) collective-permute-start(bf16[2,64,128]{2,1,0:T(8,128)(2,1)S(1)} %get-tuple-element.122), channel_id=1, source_target_pairs={{0,15},{1,0},{2,1},{3,2},{4,3},{5,4},{6,5},{7,6},{8,7},{9,8},{10,9... | collective-permute-start | bytes 98312 | tf_op jit(solution)/shard_map/while/body/eval_jaxpr/ppermute | solution.py:17
  156.5 14.0 %collective-permute-start.1 = (bf16[2,64,128]{2,1,0:T(8,128)(2,1)S(1)}, bf16[2,64,128]{2,1,0:T(8,128)(2,1)S(1)}, u32[]{:S(2)}, u32[]{:S(2)}) collective-permute-start(bf16[2,64,128]{2,1,0:T(8,128)(2,1)S(1)} %get-tuple-element.123), channel_id=1, source_target_pairs={{0,1},{1,2},{2,3},{3,4},{4,5},{5,6},{6,7},{7,8},{8,9},{9,10},{10,1... | collective-permute-start | bytes 98312 | tf_op jit(solution)/shard_map/while/body/eval_jaxpr/ppermute | solution.py:17
  158.4 12.0 %collective-permute-start.2 = (bf16[2,64,128]{2,1,0:T(8,128)(2,1)S(1)}, bf16[2,64,128]{2,1,0:T(8,128)(2,1)S(1)}, u32[]{:S(2)}, u32[]{:S(2)}) collective-permute-start(bf16[2,64,128]{2,1,0:T(8,128)(2,1)S(1)} %get-tuple-element.124), channel_id=1, source_target_pairs={{0,496},{16,0},{32,16},{48,32},{64,48},{80,64},{96,80},{112,96},{1... | collective-permute-start | bytes 98312 | tf_op jit(solution)/shard_map/while/body/eval_jaxpr/ppermute | solution.py:17
  165.1 5.4 collective-permute-start.3
  175.1 18.8 %collective-permute-start = (bf16[2,64,128]{2,1,0:T(8,128)(2,1)S(1)}, bf16[2,64,128]{2,1,0:T(8,128)(2,1)S(1)}, u32[]{:S(2)}, u32[]{:S(2)}) collective-permute-start(bf16[2,64,128]{2,1,0:T(8,128)(2,1)S(1)} %get-tuple-element.122), channel_id=1, source_target_pairs={{0,15},{1,0},{2,1},{3,2},{4,3},{5,4},{6,5},{7,6},{8,7},{9,8},{10,9... | collective-permute-start | bytes 98312 | tf_op jit(solution)/shard_map/while/body/eval_jaxpr/ppermute | solution.py:17
  179.9 14.0 %collective-permute-start.1 = (bf16[2,64,128]{2,1,0:T(8,128)(2,1)S(1)}, bf16[2,64,128]{2,1,0:T(8,128)(2,1)S(1)}, u32[]{:S(2)}, u32[]{:S(2)}) collective-permute-start(bf16[2,64,128]{2,1,0:T(8,128)(2,1)S(1)} %get-tuple-element.123), channel_id=1, source_target_pairs={{0,1},{1,2},{2,3},{3,4},{4,5},{5,6},{6,7},{7,8},{8,9},{9,10},{10,1... | collective-permute-start | bytes 98312 | tf_op jit(solution)/shard_map/while/body/eval_jaxpr/ppermute | solution.py:17
  181.8 12.0 %collective-permute-start.2 = (bf16[2,64,128]{2,1,0:T(8,128)(2,1)S(1)}, bf16[2,64,128]{2,1,0:T(8,128)(2,1)S(1)}, u32[]{:S(2)}, u32[]{:S(2)}) collective-permute-start(bf16[2,64,128]{2,1,0:T(8,128)(2,1)S(1)} %get-tuple-element.124), channel_id=1, source_target_pairs={{0,496},{16,0},{32,16},{48,32},{64,48},{80,64},{96,80},{112,96},{1... | collective-permute-start | bytes 98312 | tf_op jit(solution)/shard_map/while/body/eval_jaxpr/ppermute | solution.py:17
  188.5 5.4 collective-permute-start.3
  194.5 2.7 copy-start.1
  198.5 18.8 %collective-permute-start = (bf16[2,64,128]{2,1,0:T(8,128)(2,1)S(1)}, bf16[2,64,128]{2,1,0:T(8,128)(2,1)S(1)}, u32[]{:S(2)}, u32[]{:S(2)}) collective-permute-start(bf16[2,64,128]{2,1,0:T(8,128)(2,1)S(1)} %get-tuple-element.122), channel_id=1, source_target_pairs={{0,15},{1,0},{2,1},{3,2},{4,3},{5,4},{6,5},{7,6},{8,7},{9,8},{10,9... | collective-permute-start | bytes 98312 | tf_op jit(solution)/shard_map/while/body/eval_jaxpr/ppermute | solution.py:17
  203.3 14.0 %collective-permute-start.1 = (bf16[2,64,128]{2,1,0:T(8,128)(2,1)S(1)}, bf16[2,64,128]{2,1,0:T(8,128)(2,1)S(1)}, u32[]{:S(2)}, u32[]{:S(2)}) collective-permute-start(bf16[2,64,128]{2,1,0:T(8,128)(2,1)S(1)} %get-tuple-element.123), channel_id=1, source_target_pairs={{0,1},{1,2},{2,3},{3,4},{4,5},{5,6},{6,7},{7,8},{8,9},{9,10},{10,1... | collective-permute-start | bytes 98312 | tf_op jit(solution)/shard_map/while/body/eval_jaxpr/ppermute | solution.py:17
  205.3 12.0 %collective-permute-start.2 = (bf16[2,64,128]{2,1,0:T(8,128)(2,1)S(1)}, bf16[2,64,128]{2,1,0:T(8,128)(2,1)S(1)}, u32[]{:S(2)}, u32[]{:S(2)}) collective-permute-start(bf16[2,64,128]{2,1,0:T(8,128)(2,1)S(1)} %get-tuple-element.124), channel_id=1, source_target_pairs={{0,496},{16,0},{32,16},{48,32},{64,48},{80,64},{96,80},{112,96},{1... | collective-permute-start | bytes 98312 | tf_op jit(solution)/shard_map/while/body/eval_jaxpr/ppermute | solution.py:17
  211.9 5.4 collective-permute-start.3
  677.6 101.0 %copy-start.5 = (f32[16,64,128]{2,1,0:T(8,128)}, f32[16,64,128]{2,1,0:T(8,128)S(1)}, u32[]{:S(2)}) copy-start(f32[16,64,128]{2,1,0:T(8,128)S(1)} %broadcast_multiply_fusion) | copy-start | bytes 1572868
  (13 other events, 20.9 us)
Sparse Core Ops, SparseCore 0:
  222.3 454.0 all-reduce.2
